TPU v7x, 256 devices: a whole 4x4x8 slice. The times are simulated.
256 devices in a mesh: gx: 16 (over x, z_hi, core), gy: 4 (over z_lo), gz: 4 (over y).
Axes of the slice: x: 4, y: 4, z: 8 (z_hi: 2, z_lo: 4; z = z_hi * 4 + z_lo), core: 2. Of those that a mesh axis runs over, the one named last changes fastest.
Arguments:
- image_slab: float32 [64, 1024, 1024], P(('gz', 'gx'), None, 'gy'), may hold values from -6 to 6
- deformed_slab: float32 [64, 1024, 1024], P(('gz', 'gx'), None, 'gy'), may hold values from -6 to 6
- shifts: int32 [2, 3, 4, 16, 4], P(None, None, 'gz', 'gx', 'gy'), may hold values from -8 to 8, as said below
Outputs:
- displacement: float32 [3, 12, 144, 132], P(None, 'gz', 'gx', 'gy')
- residual_map: float32 [64, 1024, 1024], P('gz', 'gx', 'gy')
Inputs may be any that keep to these rules, and one draw needn't show every extreme that they name: `shifts`: every component lies within -8 to 8, and both ends are taken by some entry.
All inputs are finite; a program needn't handle non-finite values.
Results may differ from a plain program's by a relative error of at most 0.0003.
Values sent between devices are 32-bit elements; how exact they have to be, the bound alone decides.
No kernel may reach another device: no remote copies, remote signals or barrier semaphores. Data moves between devices by JAX's collectives and lax.ppermute only.
A program may use at most 128 MiB of HBM per device.

v0:
```python
import jax
import jax.numpy as jnp
from jax import lax
from jax.sharding import PartitionSpec as P

ELEMENT = 8
DMAX = 8
ITERS = 2
SWEEPS = 3
DAMPING = 0.7
REGULARIZE = 4.0


def padded(block, sides, width):
    for axis, dim in sides:
        count = lax.axis_size(axis)
        forward = [(i, i + 1) for i in range(count - 1)]
        backward = [(target, source) for source, target in forward]
        low = lax.ppermute(
            lax.slice_in_dim(block, block.shape[dim] - width, None, axis=dim), axis, forward
        )
        high = lax.ppermute(lax.slice_in_dim(block, 0, width, axis=dim), axis, backward)
        block = jnp.concatenate([low, block, high], axis=dim)
    return block


def node_weights(squared):
    fraction = (jnp.arange(ELEMENT, dtype=jnp.float32) + 0.5) / ELEMENT
    lower_weight = 1.0 - fraction
    if squared:
        return (lower_weight * lower_weight, fraction * fraction)
    return (lower_weight, fraction)


def weight_shape(weight, ndim, axis):
    shape = [1] * (ndim + 1)
    shape[axis + 1] = ELEMENT
    return weight.reshape(shape)


def spread_axis(nodal, axis, weights):
    count = nodal.shape[axis] - 1
    lower = jnp.expand_dims(lax.slice_in_dim(nodal, 0, count, axis=axis), axis + 1)
    upper = jnp.expand_dims(lax.slice_in_dim(nodal, 1, count + 1, axis=axis), axis + 1)
    ndim = nodal.ndim
    joined = lower * weight_shape(weights[0], ndim, axis) + upper * weight_shape(
        weights[1], ndim, axis
    )
    shape = list(nodal.shape)
    shape[axis] = count * ELEMENT
    return joined.reshape(shape)


def collect_axis(field, axis, weights):
    count = field.shape[axis] // ELEMENT
    shape = list(field.shape)
    split_shape = shape[:axis] + [count, ELEMENT] + shape[axis + 1 :]
    blocks = field.reshape(split_shape)
    ndim = field.ndim
    lower = jnp.sum(blocks * weight_shape(weights[0], ndim, axis), axis=axis + 1)
    upper = jnp.sum(blocks * weight_shape(weights[1], ndim, axis), axis=axis + 1)
    pad_low = [(0, 0)] * ndim
    pad_high = [(0, 0)] * ndim
    pad_low[axis] = (0, 1)
    pad_high[axis] = (1, 0)
    return jnp.pad(lower, pad_low) + jnp.pad(upper, pad_high)


def cut_range(array, axis, start, length):
    return lax.slice_in_dim(array, start, start + length, axis=axis)


def smooth(array, axis):
    length = array.shape[axis] - 2
    return (
        cut_range(array, axis, 0, length)
        + 2.0 * cut_range(array, axis, 1, length)
        + cut_range(array, axis, 2, length)
    ) * 0.25


def differ(array, axis):
    length = array.shape[axis] - 2
    return (cut_range(array, axis, 2, length) - cut_range(array, axis, 0, length)) * 0.5


def gradients(extended):
    along_z = smooth(smooth(differ(extended, 0), 1), 2)
    along_x = smooth(smooth(differ(extended, 1), 0), 2)
    along_y = smooth(smooth(differ(extended, 2), 0), 1)
    return jnp.stack([along_z, along_x, along_y])


def interpolate(nodal, weights):
    step = spread_axis(nodal, 3, weights)
    step = spread_axis(step, 2, weights)
    return spread_axis(step, 1, weights)


def restrict(field, weights):
    step = collect_axis(field, 1, weights)
    step = collect_axis(step, 2, weights)
    return collect_axis(step, 3, weights)


def fold_rims(extended, axis):
    moved = jnp.moveaxis(extended, axis, 0)
    inner = moved[1:-1]
    inner = inner.at[0].add(moved[0])
    inner = inner.at[-1].add(moved[-1])
    return jnp.moveaxis(inner, 0, axis)


def share(partial_value):
    extended = padded(partial_value, (("gx", 2), ("gy", 3), ("gz", 1)), 1)
    for axis in (1, 2, 3):
        extended = fold_rims(extended, axis)
    return extended


def invert(diag):
    a, b, c, d, e, f = (diag[0], diag[1], diag[2], diag[3], diag[4], diag[5])
    i00 = b * c - f * f
    i11 = a * c - e * e
    i22 = a * b - d * d
    i01 = e * f - d * c
    i02 = d * f - b * e
    i12 = d * e - a * f
    det = a * i00 + d * i01 + e * i02
    return jnp.stack([i00, i11, i22, i01, i02, i12]) / det


def apply_inverse(inverse, vector):
    out_z = inverse[0] * vector[0] + inverse[3] * vector[1] + inverse[4] * vector[2]
    out_x = inverse[3] * vector[0] + inverse[1] * vector[1] + inverse[5] * vector[2]
    out_y = inverse[4] * vector[0] + inverse[5] * vector[1] + inverse[2] * vector[2]
    return jnp.stack([out_z, out_x, out_y])


def shards(image_slab, deformed_slab, shifts):
    image, deformed_block = (
        lax.all_to_all(image_slab, "gx", split_axis=1, concat_axis=0, tiled=True),
        lax.all_to_all(deformed_slab, "gx", split_axis=1, concat_axis=0, tiled=True),
    )
    z_count, x_count, y_count = image.shape
    image_ext = padded(image, (("gx", 1), ("gy", 2), ("gz", 0)), 1)
    deformed_ext = padded(deformed_block, (("gx", 1), ("gy", 2), ("gz", 0)), DMAX)
    grads = gradients(image_ext)
    weights = node_weights(False)
    squared = node_weights(True)
    pairs = ((0, 0), (1, 1), (2, 2), (0, 1), (0, 2), (1, 2))
    products = jnp.stack([grads[i] * grads[j] for i, j in pairs])
    diag = share(restrict(products, squared))
    diag = (
        diag
        + REGULARIZE * jnp.array([1.0, 1.0, 1.0, 0.0, 0.0, 0.0], jnp.float32)[:, None, None, None]
    )
    inverse = invert(diag)
    nodal = jnp.zeros(
        (3, z_count // ELEMENT + 1, x_count // ELEMENT + 1, y_count // ELEMENT + 1), jnp.float32
    )

    def residual(nodal_now, warped_now, offset):
        moved = interpolate(nodal_now, weights)
        offset_float = offset.astype(jnp.float32)[:, None, None, None]
        return image - warped_now - jnp.sum(grads * (moved - offset_float), axis=0)

    warped = image
    offset = shifts[0, :, 0, 0, 0]
    for iteration in range(ITERS):
        offset = shifts[iteration, :, 0, 0, 0]
        starts = [DMAX + offset[0], DMAX + offset[1], DMAX + offset[2]]
        warped = lax.dynamic_slice(deformed_ext, starts, (z_count, x_count, y_count))
        resid = residual(nodal, warped, offset)
        rhs = share(restrict(grads * resid[None], weights))
        delta = DAMPING * apply_inverse(inverse, rhs)
        for sweep in range(SWEEPS - 1):
            inner = jnp.sum(grads * interpolate(delta, weights), axis=0)
            applied = share(restrict(grads * inner[None], weights)) + REGULARIZE * delta
            delta = delta + DAMPING * apply_inverse(inverse, rhs - applied)
        nodal = nodal + delta
    final = residual(nodal, warped, offset)
    return (nodal, final)


def solution(mesh):
    return jax.shard_map(
        shards,
        mesh=mesh,
        in_specs=(
            P(("gz", "gx"), None, "gy"),
            P(("gz", "gx"), None, "gy"),
            P(None, None, "gz", "gx", "gy"),
        ),
        out_specs=(P(None, "gz", "gx", "gy"), P("gz", "gx", "gy")),
        check_vma=False,
    )
```

profile of v0, /device:TPU:1, one launch (start us, length us, event | category | flops | bytes accessed | tf_op | source)
XLA Modules:
  0.0 511.1 jit_solution(6681661447291161037)
XLA Ops:
  0.6 3.4 copy.154
  4.0 12.4 %all-to-all-start = ((f32[1,1024,256]{2,0,1:T(1,128)}), f32[1,1024,256]{2,0,1:T(1,128)S(1)}, u32[]{:S(2)}, u32[]{:S(2)}) async-start(f32[1,1024,256]{2,0,1:T(1,128)} %copy.154), calls=%async_computation | async-start | bytes 2097152 | tf_op jit(solution)/shard_map/all_to_all | solution.py:142
  18.5 19.8 %all-to-all-done = f32[1,1024,256]{2,0,1:T(1,128)S(1)} async-done(((f32[1,1024,256]{2,0,1:T(1,128)}), f32[1,1024,256]{2,0,1:T(1,128)S(1)}, u32[]{:S(2)}, u32[]{:S(2)}) %all-to-all-start) | async-done | bytes 1048608 | tf_op jit(solution)/shard_map/all_to_all | solution.py:142
  38.2 5.1 all-to-all-start.1
  45.2 7.5 %collective-permute-start = (f32[16,1,256]{2,1,0:T(1,128)S(1)}, f32[16,1,256]{2,1,0:T(1,128)S(1)}, u32[]{:S(2)}, u32[]{:S(2)}) collective-permute-start(f32[16,1,256]{2,1,0:T(1,128)S(1)} %get-tuple-element.579), channel_id=1, source_target_pairs={{0,16},{16,32},{32,48},{48,64},{64,80},{80,96},{96,112},{112,128},... | collective-permute-start | bytes 49160 | tf_op jit(solution)/shard_map/ppermute | solution.py:19
  55.3 11.6 %collective-permute-done.1 = f32[16,1,256]{2,1,0:T(1,128)S(1)} collective-permute-done((f32[16,1,256]{2,1,0:T(1,128)S(1)}, f32[16,1,256]{2,1,0:T(1,128)S(1)}, u32[]{:S(2)}, u32[]{:S(2)}) %collective-permute-start.1) | collective-permute-done | bytes 16416 | tf_op jit(solution)/shard_map/ppermute | solution.py:22
  69.3 10.0 %collective-permute-start.2 = (f32[16,66,1]{1,0,2:T(8,128)S(1)}, f32[16,66,1]{1,0,2:T(8,128)S(1)}, u32[]{:S(2)}, u32[]{:S(2)}) collective-permute-start(f32[16,66,1]{1,0,2:T(8,128)S(1)} %copy.155), channel_id=1, source_target_pairs={{0,4},{4,8},{8,12},{1,5},{5,9},{9,13},{2,6},{6,10},{10,14},{3,7},{... | collective-permute-start | bytes 12680 | tf_op jit(solution)/shard_map/ppermute | solution.py:19
  88.7 4.9 collective-permute-start.5
  100.8 2.3 fusion.2
  108.2 3.5 reshape.1873
  111.8 3.3 multiply_reduce_fusion.21
  115.2 3.6 collective-permute-start.6
  120.8 6.9 %collective-permute-done.7 = f32[6,3,1,33]{3,0,2,1:T(8,128)S(1)} collective-permute-done((f32[6,3,1,33]{3,0,2,1:T(8,128)S(1)}, f32[6,3,1,33]{3,0,2,1:T(8,128)S(1)}, u32[]{:S(2)}, u32[]{:S(2)}) %collective-permute-start.7) | collective-permute-done | bytes 2408 | tf_op jit(solution)/shard_map/ppermute | solution.py:22
  127.8 4.4 collective-permute-start.8
  138.0 2.6 collective-permute-start.10
  143.6 2.5 collective-permute-done.11
  150.0 6.3 %collective-permute-start.14 = (f32[16,80,8]{1,2,0:T(8,128)S(1)}, f32[16,80,8]{1,2,0:T(8,128)S(1)}, u32[]{:S(2)}, u32[]{:S(2)}) collective-permute-start(f32[16,80,8]{1,2,0:T(8,128)S(1)} %copy.163), channel_id=1, source_target_pairs={{0,4},{4,8},{8,12},{1,5},{5,9},{9,13},{2,6},{6,10},{10,14},{3,7},{... | collective-permute-start | bytes 122888 | tf_op jit(solution)/shard_map/ppermute | solution.py:19
  160.6 2.9 collective-permute-done.15
  165.4 2.4 pad_maximum_fusion.3
  169.3 3.6 collective-permute-start.16
  179.1 3.5 scatter-add.149
  185.0 8.9 %collective-permute-done.16 = f32[8,80,272]{2,1,0:T(8,128)} collective-permute-done((f32[8,80,272]{2,1,0:T(8,128)}, f32[8,80,272]{2,1,0:T(8,128)}, u32[]{:S(2)}, u32[]{:S(2)}) %collective-permute-start.16) | collective-permute-done | bytes 696352 | tf_op jit(solution)/shard_map/ppermute | solution.py:19
  193.8 4.8 collective-permute-done.17
  198.6 3.6 pad_maximum_fusion
  208.8 8.4 %collective-permute-start.18 = (f32[3,3,1,33]{3,0,2,1:T(4,128)S(1)}, f32[3,3,1,33]{3,0,2,1:T(4,128)S(1)}, u32[]{:S(2)}, u32[]{:S(2)}) collective-permute-start(f32[3,3,1,33]{3,0,2,1:T(4,128)S(1)} %get-tuple-element.656), channel_id=1, source_target_pairs={{0,16},{16,32},{32,48},{48,64},{64,80},{80,96},{96,112},{112,128},... | collective-permute-start | bytes 3572 | tf_op jit(solution)/shard_map/ppermute | solution.py:19
  219.2 6.8 %collective-permute-done.19 = f32[3,3,1,33]{3,0,2,1:T(4,128)S(1)} collective-permute-done((f32[3,3,1,33]{3,0,2,1:T(4,128)S(1)}, f32[3,3,1,33]{3,0,2,1:T(4,128)S(1)}, u32[]{:S(2)}, u32[]{:S(2)}) %collective-permute-start.19) | collective-permute-done | bytes 1220 | tf_op jit(solution)/shard_map/ppermute | solution.py:22
  230.8 3.5 collective-permute-done.21
  238.1 3.2 collective-permute-done.23
  243.0 2.6 scatter-add.159
  252.3 2.7 mul.1701
  262.1 4.4 collective-permute-start.24
  268.6 6.8 %collective-permute-done.25 = f32[3,3,1,33]{3,0,2,1:T(4,128)S(1)} collective-permute-done((f32[3,3,1,33]{3,0,2,1:T(4,128)S(1)}, f32[3,3,1,33]{3,0,2,1:T(4,128)S(1)}, u32[]{:S(2)}, u32[]{:S(2)}) %collective-permute-start.25) | collective-permute-done | bytes 1220 | tf_op jit(solution)/shard_map/ppermute | solution.py:22
  275.6 3.5 collective-permute-start.26
  280.4 3.7 collective-permute-done.27
  284.3 3.0 collective-permute-start.28
  288.6 3.2 collective-permute-done.29
  301.8 2.7 mul.1741
  311.6 5.5 %collective-permute-start.30 = (f32[3,3,1,33]{3,0,2,1:T(4,128)S(1)}, f32[3,3,1,33]{3,0,2,1:T(4,128)S(1)}, u32[]{:S(2)}, u32[]{:S(2)}) collective-permute-start(f32[3,3,1,33]{3,0,2,1:T(4,128)S(1)} %get-tuple-element.645), channel_id=1, source_target_pairs={{0,16},{16,32},{32,48},{48,64},{64,80},{80,96},{96,112},{112,128},... | collective-permute-start | bytes 3572 | tf_op jit(solution)/shard_map/ppermute | solution.py:19
  319.2 6.8 %collective-permute-done.31 = f32[3,3,1,33]{3,0,2,1:T(4,128)S(1)} collective-permute-done((f32[3,3,1,33]{3,0,2,1:T(4,128)S(1)}, f32[3,3,1,33]{3,0,2,1:T(4,128)S(1)}, u32[]{:S(2)}, u32[]{:S(2)}) %collective-permute-start.31) | collective-permute-done | bytes 1220 | tf_op jit(solution)/shard_map/ppermute | solution.py:22
  328.9 3.7 collective-permute-done.33
  363.3 5.2 %collective-permute-start.36 = (f32[3,3,1,33]{3,0,2,1:T(4,128)S(1)}, f32[3,3,1,33]{3,0,2,1:T(4,128)S(1)}, u32[]{:S(2)}, u32[]{:S(2)}) collective-permute-start(f32[3,3,1,33]{3,0,2,1:T(4,128)S(1)} %get-tuple-element.641), channel_id=1, source_target_pairs={{0,16},{16,32},{32,48},{48,64},{64,80},{80,96},{96,112},{112,128},... | collective-permute-start | bytes 3572 | tf_op jit(solution)/shard_map/ppermute | solution.py:19
  370.6 6.8 %collective-permute-done.37 = f32[3,3,1,33]{3,0,2,1:T(4,128)S(1)} collective-permute-done((f32[3,3,1,33]{3,0,2,1:T(4,128)S(1)}, f32[3,3,1,33]{3,0,2,1:T(4,128)S(1)}, u32[]{:S(2)}, u32[]{:S(2)}) %collective-permute-start.37) | collective-permute-done | bytes 1220 | tf_op jit(solution)/shard_map/ppermute | solution.py:22
  380.2 3.7 collective-permute-done.39
  384.0 3.2 collective-permute-start.40
  388.5 3.2 collective-permute-done.41
  392.6 2.3 scatter-add.189
  396.7 2.7 mul.1810
  400.9 2.7 mul.1813
  407.3 2.7 reshape.1883
  412.3 4.8 collective-permute-start.42
  419.1 6.8 %collective-permute-done.43 = f32[3,3,1,33]{3,0,2,1:T(4,128)S(1)} collective-permute-done((f32[3,3,1,33]{3,0,2,1:T(4,128)S(1)}, f32[3,3,1,33]{3,0,2,1:T(4,128)S(1)}, u32[]{:S(2)}, u32[]{:S(2)}) %collective-permute-start.43) | collective-permute-done | bytes 1220 | tf_op jit(solution)/shard_map/ppermute | solution.py:22
  429.3 3.7 collective-permute-done.45
  435.8 3.2 collective-permute-done.47
  441.9 3.3 scatter-add.199
  447.7 2.7 mul.1846
  452.0 2.7 mul.1849
  458.4 2.7 reshape.1885
  463.4 4.8 collective-permute-start.48
  470.2 6.8 %collective-permute-done.49 = f32[3,3,1,33]{3,0,2,1:T(4,128)S(1)} collective-permute-done((f32[3,3,1,33]{3,0,2,1:T(4,128)S(1)}, f32[3,3,1,33]{3,0,2,1:T(4,128)S(1)}, u32[]{:S(2)}, u32[]{:S(2)}) %collective-permute-start.49) | collective-permute-done | bytes 1220 | tf_op jit(solution)/shard_map/ppermute | solution.py:22
  480.1 3.7 collective-permute-done.51
  483.9 2.5 collective-permute-start.52
  487.7 3.2 collective-permute-done.53
  493.8 2.8 scatter-add.209
  508.1 2.8 bitcast_subtract_fusion
  (484 shorter events, 201.2 us)
Async XLA Ops:
  4.0 34.2 %all-to-all-start = ((f32[1,1024,256]{2,0,1:T(1,128)}), f32[1,1024,256]{2,0,1:T(1,128)S(1)}, u32[]{:S(2)}, u32[]{:S(2)}) async-start(f32[1,1024,256]{2,0,1:T(1,128)} %copy.154), calls=%async_computation | async-start | bytes 2097152 | tf_op jit(solution)/shard_map/all_to_all | solution.py:142
  18.5 36.1 %copy-start.44 = (s32[2,3,1,1,1]{1,4,3,2,0:T(1,128)S(1)}, s32[2,3,1,1,1]{1,4,3,2,0:T(1,128)}, u32[]{:S(2)}) copy-start(s32[2,3,1,1,1]{1,4,3,2,0:T(1,128)} %param.90) | copy-start | bytes 76
  38.2 55.3 %all-to-all-start.1 = ((f32[1,1024,256]{2,0,1:T(1,128)}), f32[1,1024,256]{2,0,1:T(1,128)}, u32[]{:S(2)}, u32[]{:S(2)}) async-start(f32[1,1024,256]{2,0,1:T(1,128)} %copy.162), calls=%async_computation.1 | async-start | bytes 2097152 | tf_op jit(solution)/shard_map/all_to_all | solution.py:143
  45.1 54.6 %copy-start = (f32[1,1024,256]{2,1,0:T(8,128)}, f32[1,1024,256]{2,1,0:T(8,128)S(1)}, u32[]{:S(2)}) copy-start(f32[1,1024,256]{2,1,0:T(8,128)S(1)} %copy.210) | copy-start | bytes 3145732
  45.2 10.1 %collective-permute-start = (f32[16,1,256]{2,1,0:T(1,128)S(1)}, f32[16,1,256]{2,1,0:T(1,128)S(1)}, u32[]{:S(2)}, u32[]{:S(2)}) collective-permute-start(f32[16,1,256]{2,1,0:T(1,128)S(1)} %get-tuple-element.579), channel_id=1, source_target_pairs={{0,16},{16,32},{32,48},{48,64},{64,80},{80,96},{96,112},{112,128},... | collective-permute-start | bytes 49160 | tf_op jit(solution)/shard_map/ppermute | solution.py:19
  52.6 14.2 %collective-permute-start.1 = (f32[16,1,256]{2,1,0:T(1,128)S(1)}, f32[16,1,256]{2,1,0:T(1,128)S(1)}, u32[]{:S(2)}, u32[]{:S(2)}) collective-permute-start(f32[16,1,256]{2,1,0:T(1,128)S(1)} %get-tuple-element.580), channel_id=1, source_target_pairs={{16,0},{32,16},{48,32},{64,48},{80,64},{96,80},{112,96},{128,112},... | collective-permute-start | bytes 49160 | tf_op jit(solution)/shard_map/ppermute | solution.py:22
  69.3 17.2 %collective-permute-start.2 = (f32[16,66,1]{1,0,2:T(8,128)S(1)}, f32[16,66,1]{1,0,2:T(8,128)S(1)}, u32[]{:S(2)}, u32[]{:S(2)}) collective-permute-start(f32[16,66,1]{1,0,2:T(8,128)S(1)} %copy.155), channel_id=1, source_target_pairs={{0,4},{4,8},{8,12},{1,5},{5,9},{9,13},{2,6},{6,10},{10,14},{3,7},{... | collective-permute-start | bytes 12680 | tf_op jit(solution)/shard_map/ppermute | solution.py:19
  79.6 7.3 %collective-permute-start.3 = (f32[16,66,1]{1,0,2:T(8,128)S(1)}, f32[16,66,1]{1,0,2:T(8,128)S(1)}, u32[]{:S(2)}, u32[]{:S(2)}) collective-permute-start(f32[16,66,1]{1,0,2:T(8,128)S(1)} %copy.156), channel_id=1, source_target_pairs={{4,0},{8,4},{12,8},{5,1},{9,5},{13,9},{6,2},{10,6},{14,10},{7,3},{... | collective-permute-start | bytes 12680 | tf_op jit(solution)/shard_map/ppermute | solution.py:22
  87.4 8.5 %collective-permute-start.4 = (f32[1,66,258]{2,1,0:T(8,128)S(1)}, f32[1,66,258]{2,1,0:T(8,128)S(1)}, u32[]{:S(2)}, u32[]{:S(2)}) collective-permute-start(f32[1,66,258]{2,1,0:T(8,128)S(1)} %get-tuple-element.566), channel_id=1, source_target_pairs={{1,0},{2,1},{3,2},{5,4},{6,5},{7,6},{9,8},{10,9},{11,10},{13,12},{... | collective-permute-start | bytes 204344 | tf_op jit(solution)/shard_map/ppermute | solution.py:22
  88.7 7.8 %collective-permute-start.5 = (f32[1,66,258]{2,1,0:T(8,128)S(1)}, f32[1,66,258]{2,1,0:T(8,128)}, u32[]{:S(2)}, u32[]{:S(2)}) collective-permute-start(f32[1,66,258]{2,1,0:T(8,128)S(1)} %get-tuple-element.565), channel_id=1, source_target_pairs={{0,1},{1,2},{2,3},{4,5},{5,6},{6,7},{8,9},{9,10},{10,11},{12,13},{... | collective-permute-start | bytes 204344 | tf_op jit(solution)/shard_map/ppermute | solution.py:19
  111.8 30.1 %copy-start.11 = (f32[3,2,64,256]{3,2,1,0:T(8,128)S(1)}, f32[3,2,64,256]{3,2,1,0:T(8,128)}, u32[]{:S(2)}) copy-start(f32[3,2,64,256]{3,2,1,0:T(8,128)} %get-tuple-element.594) | copy-start | bytes 1179652
  111.8 30.2 %copy-start.46 = (f32[3]{0:T(128)S(1)}, f32[3]{0:T(128)}, u32[]{:S(2)}) copy-start(f32[3]{0:T(128)} %get-tuple-element.689) | copy-start | bytes 40
  115.2 5.6 %collective-permute-start.6 = (f32[6,3,1,33]{3,0,2,1:T(8,128)S(1)}, f32[6,3,1,33]{3,0,2,1:T(8,128)S(1)}, u32[]{:S(2)}, u32[]{:S(2)}) collective-permute-start(f32[6,3,1,33]{3,0,2,1:T(8,128)S(1)} %get-tuple-element.597), channel_id=1, source_target_pairs={{0,16},{16,32},{32,48},{48,64},{64,80},{80,96},{96,112},{112,128},... | collective-permute-start | bytes 7136 | tf_op jit(solution)/shard_map/ppermute | solution.py:19
  118.7 8.9 %collective-permute-start.7 = (f32[6,3,1,33]{3,0,2,1:T(8,128)S(1)}, f32[6,3,1,33]{3,0,2,1:T(8,128)S(1)}, u32[]{:S(2)}, u32[]{:S(2)}) collective-permute-start(f32[6,3,1,33]{3,0,2,1:T(8,128)S(1)} %get-tuple-element.598), channel_id=1, source_target_pairs={{16,0},{32,16},{48,32},{64,48},{80,64},{96,80},{112,96},{128,112},... | collective-permute-start | bytes 7136 | tf_op jit(solution)/shard_map/ppermute | solution.py:22
  127.8 10.1 %collective-permute-start.8 = (f32[6,3,11,1]{3,0,2,1:T(8,128)S(1)}, f32[6,3,11,1]{3,0,2,1:T(8,128)S(1)}, u32[]{:S(2)}, u32[]{:S(2)}) collective-permute-start(f32[6,3,11,1]{3,0,2,1:T(8,128)S(1)} %get-tuple-element.629), channel_id=1, source_target_pairs={{0,4},{4,8},{8,12},{1,5},{5,9},{9,13},{2,6},{6,10},{10,14},{3,7},{... | collective-permute-start | bytes 2384 | tf_op jit(solution)/shard_map/ppermute | solution.py:19
  132.1 5.8 %collective-permute-start.9 = (f32[6,3,11,1]{3,0,2,1:T(8,128)S(1)}, f32[6,3,11,1]{3,0,2,1:T(8,128)S(1)}, u32[]{:S(2)}, u32[]{:S(2)}) collective-permute-start(f32[6,3,11,1]{3,0,2,1:T(8,128)S(1)} %get-tuple-element.630), channel_id=1, source_target_pairs={{4,0},{8,4},{12,8},{5,1},{9,5},{13,9},{6,2},{10,6},{14,10},{7,3},{... | collective-permute-start | bytes 2384 | tf_op jit(solution)/shard_map/ppermute | solution.py:22
  133.5 12.8 %collective-permute-start.12 = (f32[16,8,256]{2,1,0:T(8,128)S(1)}, f32[16,8,256]{2,1,0:T(8,128)S(1)}, u32[]{:S(2)}, u32[]{:S(2)}) collective-permute-start(f32[16,8,256]{2,1,0:T(8,128)S(1)} %get-tuple-element.577), channel_id=1, source_target_pairs={{0,16},{16,32},{32,48},{48,64},{64,80},{80,96},{96,112},{112,128},... | collective-permute-start | bytes 393224 | tf_op jit(solution)/shard_map/ppermute | solution.py:19
  135.6 11.7 %collective-permute-start.13 = (f32[16,8,256]{2,1,0:T(8,128)S(1)}, f32[16,8,256]{2,1,0:T(8,128)S(1)}, u32[]{:S(2)}, u32[]{:S(2)}) collective-permute-start(f32[16,8,256]{2,1,0:T(8,128)S(1)} %get-tuple-element.578), channel_id=1, source_target_pairs={{16,0},{32,16},{48,32},{64,48},{80,64},{96,80},{112,96},{128,112},... | collective-permute-start | bytes 393224 | tf_op jit(solution)/shard_map/ppermute | solution.py:22
  138.0 5.6 %collective-permute-start.10 = (f32[6,1,11,35]{3,0,2,1:T(8,128)S(1)}, f32[6,1,11,35]{3,0,2,1:T(8,128)S(1)}, u32[]{:S(2)}, u32[]{:S(2)}) collective-permute-start(f32[6,1,11,35]{3,0,2,1:T(8,128)S(1)} %get-tuple-element.595), channel_id=1, source_target_pairs={{0,1},{1,2},{2,3},{4,5},{5,6},{6,7},{8,9},{9,10},{10,11},{12,13},{... | collective-permute-start | bytes 27728 | tf_op jit(solution)/shard_map/ppermute | solution.py:19
  140.6 5.5 %collective-permute-start.11 = (f32[6,1,11,35]{3,0,2,1:T(8,128)S(1)}, f32[6,1,11,35]{3,0,2,1:T(8,128)S(1)}, u32[]{:S(2)}, u32[]{:S(2)}) collective-permute-start(f32[6,1,11,35]{3,0,2,1:T(8,128)S(1)} %get-tuple-element.596), channel_id=1, source_target_pairs={{1,0},{2,1},{3,2},{5,4},{6,5},{7,6},{9,8},{10,9},{11,10},{13,12},{... | collective-permute-start | bytes 27728 | tf_op jit(solution)/shard_map/ppermute | solution.py:22
  150.0 9.5 %collective-permute-start.14 = (f32[16,80,8]{1,2,0:T(8,128)S(1)}, f32[16,80,8]{1,2,0:T(8,128)S(1)}, u32[]{:S(2)}, u32[]{:S(2)}) collective-permute-start(f32[16,80,8]{1,2,0:T(8,128)S(1)} %copy.163), channel_id=1, source_target_pairs={{0,4},{4,8},{8,12},{1,5},{5,9},{9,13},{2,6},{6,10},{10,14},{3,7},{... | collective-permute-start | bytes 122888 | tf_op jit(solution)/shard_map/ppermute | solution.py:19
  158.2 5.3 %collective-permute-start.15 = (f32[16,80,8]{1,2,0:T(8,128)}, f32[16,80,8]{1,2,0:T(8,128)}, u32[]{:S(2)}, u32[]{:S(2)}) collective-permute-start(f32[16,80,8]{1,2,0:T(8,128)} %copy.164), channel_id=1, source_target_pairs={{4,0},{8,4},{12,8},{5,1},{9,5},{13,9},{6,2},{10,6},{14,10},{7,3},{... | collective-permute-start | bytes 122888 | tf_op jit(solution)/shard_map/ppermute | solution.py:22
  167.9 30.8 %copy-start.13 = (f32[16,8,256]{2,1,0:T(8,128)S(1)}, f32[16,8,256]{2,1,0:T(8,128)}, u32[]{:S(2)}) copy-start(f32[16,8,256]{2,1,0:T(8,128)} %copy-done.12) | copy-start | bytes 393220
  167.9 30.8 %copy-start.15 = (f32[16,8,256]{2,1,0:T(8,128)S(1)}, f32[16,8,256]{2,1,0:T(8,128)}, u32[]{:S(2)}) copy-start(f32[16,8,256]{2,1,0:T(8,128)} %copy-done.14) | copy-start | bytes 393220
  169.3 24.5 %collective-permute-start.16 = (f32[8,80,272]{2,1,0:T(8,128)}, f32[8,80,272]{2,1,0:T(8,128)}, u32[]{:S(2)}, u32[]{:S(2)}) collective-permute-start(f32[8,80,272]{2,1,0:T(8,128)} %get-tuple-element.570), channel_id=1, source_target_pairs={{0,1},{1,2},{2,3},{4,5},{5,6},{6,7},{8,9},{9,10},{10,11},{12,13},{... | collective-permute-start | bytes 2088968 | tf_op jit(solution)/shard_map/ppermute | solution.py:19
  172.9 25.7 %collective-permute-start.17 = (f32[8,80,272]{2,1,0:T(8,128)}, f32[8,80,272]{2,1,0:T(8,128)}, u32[]{:S(2)}, u32[]{:S(2)}) collective-permute-start(f32[8,80,272]{2,1,0:T(8,128)} %get-tuple-element.571), channel_id=1, source_target_pairs={{1,0},{2,1},{3,2},{5,4},{6,5},{7,6},{9,8},{10,9},{11,10},{13,12},{... | collective-permute-start | bytes 2088968 | tf_op jit(solution)/shard_map/ppermute | solution.py:22
  204.2 25.7 %copy-start.31 = (f32[1,3,9,33]{3,0,2,1:T(1,128)S(1)}, f32[1,3,9,33]{3,0,2,1:T(1,128)}, u32[]{:S(2)}) copy-start(f32[1,3,9,33]{3,0,2,1:T(1,128)} %get-tuple-element.557) | copy-start | bytes 10696
  204.2 33.9 %copy-start.30 = (f32[3,9,33]{2,1,0:T(8,128)S(1)}, f32[3,9,33]{2,1,0:T(8,128)}, u32[]{:S(2)}) copy-start(f32[3,9,33]{2,1,0:T(8,128)} %copy.161) | copy-start | bytes 10696
  208.8 10.4 %collective-permute-start.18 = (f32[3,3,1,33]{3,0,2,1:T(4,128)S(1)}, f32[3,3,1,33]{3,0,2,1:T(4,128)S(1)}, u32[]{:S(2)}, u32[]{:S(2)}) collective-permute-start(f32[3,3,1,33]{3,0,2,1:T(4,128)S(1)} %get-tuple-element.656), channel_id=1, source_target_pairs={{0,16},{16,32},{32,48},{48,64},{64,80},{80,96},{96,112},{112,128},... | collective-permute-start | bytes 3572 | tf_op jit(solution)/shard_map/ppermute | solution.py:19
  217.2 8.9 %collective-permute-start.19 = (f32[3,3,1,33]{3,0,2,1:T(4,128)S(1)}, f32[3,3,1,33]{3,0,2,1:T(4,128)S(1)}, u32[]{:S(2)}, u32[]{:S(2)}) collective-permute-start(f32[3,3,1,33]{3,0,2,1:T(4,128)S(1)} %get-tuple-element.657), channel_id=1, source_target_pairs={{16,0},{32,16},{48,32},{64,48},{80,64},{96,80},{112,96},{128,112},... | collective-permute-start | bytes 3572 | tf_op jit(solution)/shard_map/ppermute | solution.py:22
  226.8 4.0 collective-permute-start.20
  228.6 5.7 %collective-permute-start.21 = (f32[3,3,11,1]{3,0,2,1:T(4,128)}, f32[3,3,11,1]{3,0,2,1:T(4,128)S(1)}, u32[]{:S(2)}, u32[]{:S(2)}) collective-permute-start(f32[3,3,11,1]{3,0,2,1:T(4,128)} %get-tuple-element.669), channel_id=1, source_target_pairs={{4,0},{8,4},{12,8},{5,1},{9,5},{13,9},{6,2},{10,6},{14,10},{7,3},{... | collective-permute-start | bytes 1196 | tf_op jit(solution)/shard_map/ppermute | solution.py:22
  234.4 3.6 collective-permute-start.22
  236.7 4.5 collective-permute-start.23
  262.1 6.5 %collective-permute-start.24 = (f32[3,3,1,33]{3,0,2,1:T(4,128)S(1)}, f32[3,3,1,33]{3,0,2,1:T(4,128)S(1)}, u32[]{:S(2)}, u32[]{:S(2)}) collective-permute-start(f32[3,3,1,33]{3,0,2,1:T(4,128)S(1)} %get-tuple-element.649), channel_id=1, source_target_pairs={{0,16},{16,32},{32,48},{48,64},{64,80},{80,96},{96,112},{112,128},... | collective-permute-start | bytes 3572 | tf_op jit(solution)/shard_map/ppermute | solution.py:19
  266.6 8.9 %collective-permute-start.25 = (f32[3,3,1,33]{3,0,2,1:T(4,128)S(1)}, f32[3,3,1,33]{3,0,2,1:T(4,128)S(1)}, u32[]{:S(2)}, u32[]{:S(2)}) collective-permute-start(f32[3,3,1,33]{3,0,2,1:T(4,128)S(1)} %get-tuple-element.650), channel_id=1, source_target_pairs={{16,0},{32,16},{48,32},{64,48},{80,64},{96,80},{112,96},{128,112},... | collective-permute-start | bytes 3572 | tf_op jit(solution)/shard_map/ppermute | solution.py:22
  275.6 4.9 collective-permute-start.26
  279.1 5.0 collective-permute-start.27
  284.3 4.3 collective-permute-start.28
  287.3 4.5 collective-permute-start.29
  311.6 7.6 %collective-permute-start.30 = (f32[3,3,1,33]{3,0,2,1:T(4,128)S(1)}, f32[3,3,1,33]{3,0,2,1:T(4,128)S(1)}, u32[]{:S(2)}, u32[]{:S(2)}) collective-permute-start(f32[3,3,1,33]{3,0,2,1:T(4,128)S(1)} %get-tuple-element.645), channel_id=1, source_target_pairs={{0,16},{16,32},{32,48},{48,64},{64,80},{80,96},{96,112},{112,128},... | collective-permute-start | bytes 3572 | tf_op jit(solution)/shard_map/ppermute | solution.py:19
  317.1 8.9 %collective-permute-start.31 = (f32[3,3,1,33]{3,0,2,1:T(4,128)S(1)}, f32[3,3,1,33]{3,0,2,1:T(4,128)S(1)}, u32[]{:S(2)}, u32[]{:S(2)}) collective-permute-start(f32[3,3,1,33]{3,0,2,1:T(4,128)S(1)} %get-tuple-element.646), channel_id=1, source_target_pairs={{16,0},{32,16},{48,32},{64,48},{80,64},{96,80},{112,96},{128,112},... | collective-permute-start | bytes 3572 | tf_op jit(solution)/shard_map/ppermute | solution.py:22
  326.1 2.8 collective-permute-start.32
  327.6 5.0 collective-permute-start.33
  334.0 6.5 %collective-permute-start.34 = (f32[3,1,11,35]{3,0,2,1:T(4,128)}, f32[3,1,11,35]{3,0,2,1:T(4,128)S(1)}, u32[]{:S(2)}, u32[]{:S(2)}) collective-permute-start(f32[3,1,11,35]{3,0,2,1:T(4,128)} %get-tuple-element.605), channel_id=1, source_target_pairs={{0,1},{1,2},{2,3},{4,5},{5,6},{6,7},{8,9},{9,10},{10,11},{12,13},{... | collective-permute-start | bytes 13868 | tf_op jit(solution)/shard_map/ppermute | solution.py:19
  335.7 4.9 collective-permute-start.35
  363.3 7.2 %collective-permute-start.36 = (f32[3,3,1,33]{3,0,2,1:T(4,128)S(1)}, f32[3,3,1,33]{3,0,2,1:T(4,128)S(1)}, u32[]{:S(2)}, u32[]{:S(2)}) collective-permute-start(f32[3,3,1,33]{3,0,2,1:T(4,128)S(1)} %get-tuple-element.641), channel_id=1, source_target_pairs={{0,16},{16,32},{32,48},{48,64},{64,80},{80,96},{96,112},{112,128},... | collective-permute-start | bytes 3572 | tf_op jit(solution)/shard_map/ppermute | solution.py:19
  368.5 8.9 %collective-permute-start.37 = (f32[3,3,1,33]{3,0,2,1:T(4,128)S(1)}, f32[3,3,1,33]{3,0,2,1:T(4,128)S(1)}, u32[]{:S(2)}, u32[]{:S(2)}) collective-permute-start(f32[3,3,1,33]{3,0,2,1:T(4,128)S(1)} %get-tuple-element.642), channel_id=1, source_target_pairs={{16,0},{32,16},{48,32},{64,48},{80,64},{96,80},{112,96},{128,112},... | collective-permute-start | bytes 3572 | tf_op jit(solution)/shard_map/ppermute | solution.py:22
  377.5 2.7 collective-permute-start.38
  378.9 5.0 collective-permute-start.39
  384.0 4.5 collective-permute-start.40
  387.2 4.5 collective-permute-start.41
  412.3 6.8 %collective-permute-start.42 = (f32[3,3,1,33]{3,0,2,1:T(4,128)S(1)}, f32[3,3,1,33]{3,0,2,1:T(4,128)S(1)}, u32[]{:S(2)}, u32[]{:S(2)}) collective-permute-start(f32[3,3,1,33]{3,0,2,1:T(4,128)S(1)} %get-tuple-element.637), channel_id=1, source_target_pairs={{0,16},{16,32},{32,48},{48,64},{64,80},{80,96},{96,112},{112,128},... | collective-permute-start | bytes 3572 | tf_op jit(solution)/shard_map/ppermute | solution.py:19
  417.1 8.9 %collective-permute-start.43 = (f32[3,3,1,33]{3,0,2,1:T(4,128)S(1)}, f32[3,3,1,33]{3,0,2,1:T(4,128)S(1)}, u32[]{:S(2)}, u32[]{:S(2)}) collective-permute-start(f32[3,3,1,33]{3,0,2,1:T(4,128)S(1)} %get-tuple-element.638), channel_id=1, source_target_pairs={{16,0},{32,16},{48,32},{64,48},{80,64},{96,80},{112,96},{128,112},... | collective-permute-start | bytes 3572 | tf_op jit(solution)/shard_map/ppermute | solution.py:22
  426.0 3.2 collective-permute-start.44
  427.9 5.0 collective-permute-start.45
  433.1 2.7 collective-permute-start.46
  434.5 4.5 collective-permute-start.47
  463.4 6.8 %collective-permute-start.48 = (f32[3,3,1,33]{3,0,2,1:T(4,128)S(1)}, f32[3,3,1,33]{3,0,2,1:T(4,128)S(1)}, u32[]{:S(2)}, u32[]{:S(2)}) collective-permute-start(f32[3,3,1,33]{3,0,2,1:T(4,128)S(1)} %get-tuple-element.633), channel_id=1, source_target_pairs={{0,16},{16,32},{32,48},{48,64},{64,80},{80,96},{96,112},{112,128},... | collective-permute-start | bytes 3572 | tf_op jit(solution)/shard_map/ppermute | solution.py:19
  468.2 8.9 %collective-permute-start.49 = (f32[3,3,1,33]{3,0,2,1:T(4,128)S(1)}, f32[3,3,1,33]{3,0,2,1:T(4,128)S(1)}, u32[]{:S(2)}, u32[]{:S(2)}) collective-permute-start(f32[3,3,1,33]{3,0,2,1:T(4,128)S(1)} %get-tuple-element.634), channel_id=1, source_target_pairs={{16,0},{32,16},{48,32},{64,48},{80,64},{96,80},{112,96},{128,112},... | collective-permute-start | bytes 3572 | tf_op jit(solution)/shard_map/ppermute | solution.py:22
  477.1 3.0 collective-permute-start.50
  478.8 5.0 collective-permute-start.51
  483.9 3.8 collective-permute-start.52
  486.4 4.5 collective-permute-start.53
  (40 other events, 223.2 us)
where the time goes:
time: 519 us; the launch traced here: 511 us
  starting transfers between devices  162 us (31%)
  waiting for transfers between devices  138 us (27%)
  local copies, waits for them, and re-layouts  127 us (24%)
  other arithmetic  74.1 us (14%)
  between operations  10.8 us (2%)
    ppermute x27, waiting for transfers between devices, padded(): lax.ppermute(lax.slice_in_dim(block, 0, width, axis=dim), axis, backward)  109 us
    ppermute x27, starting transfers between devices, padded(): lax.ppermute(lax.slice_in_dim(block, block.shape[dim] - width, None, axis...  104 us
    ppermute x27, starting transfers between devices, padded(): lax.ppermute(lax.slice_in_dim(block, 0, width, axis=dim), axis, backward)  40.8 us
    mul x16, local copies, waits for them, and re-layouts, spread_axis(): upper * weight_shape(weights[1], ndim, axis)  24.5 us
    mul x17, local copies, waits for them, and re-layouts, spread_axis(): lower * weight_shape(weights[0], ndim, axis)  23.2 us
    all_to_all x1, waiting for transfers between devices, shards(): lax.all_to_all(image_slab, 'gx', split_axis=1, concat_axis=0, tiled=True)  19.8 us
    scatter-add x7, local copies, waits for them, and re-layouts, fold_rims(): inner = inner.at[-1].add(moved[-1])  18.9 us
    reshape x7, local copies, waits for them, and re-layouts, collect_axis(): blocks = field.reshape(split_shape)  16.3 us
  transfers between devices with their start and end apart: 56, of which 27 were waited for; matrix products, arithmetic and copies ran while one was open for 6% of the time, Pallas kernels for 0%

commit v1 on v0

--- a/solution.py
+++ b/solution.py
@@ -138,8 +138,20 @@
 
 
 def shards(image_slab, deformed_slab, shifts):
+
+    def _advance_strips_all(my_data):
+        return jnp.concatenate(
+            lax.all_to_all(
+                jnp.stack(jnp.split(my_data, lax.axis_size("gx"), 1), 0),
+                concat_axis=0,
+                split_axis=0,
+                axis_name="gx",
+            ),
+            0,
+        )
+
     image, deformed_block = (
-        lax.all_to_all(image_slab, "gx", split_axis=1, concat_axis=0, tiled=True),
+        _advance_strips_all(image_slab),
         lax.all_to_all(deformed_slab, "gx", split_axis=1, concat_axis=0, tiled=True),
     )
     z_count, x_count, y_count = image.shape

time: 519 us -> 539 us (1.039)
  local copies, waits for them, and re-layouts: 127 us -> 147 us
    unnamed x106 -> x119, local copies, waits for them, and re-layouts: 14.1 us -> 32.9 us
  transfers between devices with their start and end apart: 56 -> 56, of which waited for: 27 -> 27; matrix products, arithmetic and copies ran while one was open for 6% -> 5% of each run, Pallas kernels for 0% -> 0%
where the time goes in v1:
time: 539 us; the launch traced here: 531 us
  starting transfers between devices  162 us (30%)
  local copies, waits for them, and re-layouts  147 us (27%)
  waiting for transfers between devices  138 us (26%)
  other arithmetic  74.1 us (14%)
  between operations  10.8 us (2%)
    ppermute x27, waiting for transfers between devices, padded(): lax.ppermute(lax.slice_in_dim(block, 0, width, axis=dim), axis, backward)  109 us
    ppermute x27, starting transfers between devices, padded(): lax.ppermute(lax.slice_in_dim(block, block.shape[dim] - width, None, axis...  104 us
    ppermute x27, starting transfers between devices, padded(): lax.ppermute(lax.slice_in_dim(block, 0, width, axis=dim), axis, backward)  40.8 us
    unnamed x119, local copies, waits for them, and re-layouts  32.9 us
    mul x16, local copies, waits for them, and re-layouts, spread_axis(): upper * weight_shape(weights[1], ndim, axis)  24.5 us
    mul x17, local copies, waits for them, and re-layouts, spread_axis(): lower * weight_shape(weights[0], ndim, axis)  23.2 us
    all_to_all x1, waiting for transfers between devices, _advance_strips_all(): lax.all_to_all(jnp.stack(jnp.split(my_data, lax.axis_size('gx'), 1), 0),...  19.7 us
    scatter-add x7, local copies, waits for them, and re-layouts, fold_rims(): inner = inner.at[-1].add(moved[-1])  18.9 us
  transfers between devices with their start and end apart: 56, of which 27 were waited for; matrix products, arithmetic and copies ran while one was open for 5% of the time, Pallas kernels for 0%

profile of v1, /device:TPU:1, one launch (start us, length us, event | category | flops | bytes accessed | tf_op | source)
XLA Modules:
  0.0 531.4 jit_solution(888674407057983331)
XLA Ops:
  24.3 12.4 %all-to-all-start = ((f32[16,1,64,256]{3,2,1,0:T(8,128)}), f32[16,1,64,256]{3,2,1,0:T(8,128)S(1)}, u32[]{:S(2)}, u32[]{:S(2)}) async-start(f32[16,1,64,256]{3,2,1,0:T(8,128)} %bitcast_dynamic-update-slice_fusion), calls=%async_computation | async-start | bytes 2097152 | tf_op jit(solution)/shard_map/all_to_all | solution.py:144
  38.8 19.7 %all-to-all-done = f32[16,1,64,256]{3,2,1,0:T(8,128)S(1)} async-done(((f32[16,1,64,256]{3,2,1,0:T(8,128)}), f32[16,1,64,256]{3,2,1,0:T(8,128)S(1)}, u32[]{:S(2)}, u32[]{:S(2)}) %all-to-all-start) | async-done | bytes 1048608 | tf_op jit(solution)/shard_map/all_to_all | solution.py:144
  58.5 5.1 all-to-all-start.1
  65.4 7.5 %collective-permute-start = (f32[16,1,256]{2,1,0:T(1,128)S(1)}, f32[16,1,256]{2,1,0:T(1,128)S(1)}, u32[]{:S(2)}, u32[]{:S(2)}) collective-permute-start(f32[16,1,256]{2,1,0:T(1,128)S(1)} %get-tuple-element.579), channel_id=1, source_target_pairs={{0,16},{16,32},{32,48},{48,64},{64,80},{80,96},{96,112},{112,128},... | collective-permute-start | bytes 49160 | tf_op jit(solution)/shard_map/ppermute | solution.py:19
  75.6 11.6 %collective-permute-done.1 = f32[16,1,256]{2,1,0:T(1,128)S(1)} collective-permute-done((f32[16,1,256]{2,1,0:T(1,128)S(1)}, f32[16,1,256]{2,1,0:T(1,128)S(1)}, u32[]{:S(2)}, u32[]{:S(2)}) %collective-permute-start.1) | collective-permute-done | bytes 16416 | tf_op jit(solution)/shard_map/ppermute | solution.py:22
  89.6 10.0 %collective-permute-start.2 = (f32[16,66,1]{1,0,2:T(8,128)S(1)}, f32[16,66,1]{1,0,2:T(8,128)S(1)}, u32[]{:S(2)}, u32[]{:S(2)}) collective-permute-start(f32[16,66,1]{1,0,2:T(8,128)S(1)} %copy.148), channel_id=1, source_target_pairs={{0,4},{4,8},{8,12},{1,5},{5,9},{9,13},{2,6},{6,10},{10,14},{3,7},{... | collective-permute-start | bytes 12680 | tf_op jit(solution)/shard_map/ppermute | solution.py:19
  109.0 4.9 collective-permute-start.5
  113.9 2.3 copy.203
  121.1 2.3 fusion.2
  128.5 3.5 reshape.1874
  132.1 3.3 multiply_reduce_fusion.21
  135.5 3.5 collective-permute-start.6
  141.0 6.9 %collective-permute-done.7 = f32[6,3,1,33]{3,0,2,1:T(8,128)S(1)} collective-permute-done((f32[6,3,1,33]{3,0,2,1:T(8,128)S(1)}, f32[6,3,1,33]{3,0,2,1:T(8,128)S(1)}, u32[]{:S(2)}, u32[]{:S(2)}) %collective-permute-start.7) | collective-permute-done | bytes 2408 | tf_op jit(solution)/shard_map/ppermute | solution.py:22
  148.0 4.4 collective-permute-start.8
  158.3 2.6 collective-permute-start.10
  163.9 2.5 collective-permute-done.11
  170.3 6.3 %collective-permute-start.14 = (f32[16,80,8]{1,2,0:T(8,128)S(1)}, f32[16,80,8]{1,2,0:T(8,128)S(1)}, u32[]{:S(2)}, u32[]{:S(2)}) collective-permute-start(f32[16,80,8]{1,2,0:T(8,128)S(1)} %copy.156), channel_id=1, source_target_pairs={{0,4},{4,8},{8,12},{1,5},{5,9},{9,13},{2,6},{6,10},{10,14},{3,7},{... | collective-permute-start | bytes 122888 | tf_op jit(solution)/shard_map/ppermute | solution.py:19
  180.9 2.9 collective-permute-done.15
  185.7 2.4 pad_maximum_fusion.3
  189.6 3.6 collective-permute-start.16
  199.3 3.5 scatter-add.149
  205.3 8.9 %collective-permute-done.16 = f32[8,80,272]{2,1,0:T(8,128)} collective-permute-done((f32[8,80,272]{2,1,0:T(8,128)}, f32[8,80,272]{2,1,0:T(8,128)}, u32[]{:S(2)}, u32[]{:S(2)}) %collective-permute-start.16) | collective-permute-done | bytes 696352 | tf_op jit(solution)/shard_map/ppermute | solution.py:19
  214.1 4.8 collective-permute-done.17
  218.9 3.6 pad_maximum_fusion
  229.1 8.4 %collective-permute-start.18 = (f32[3,3,1,33]{3,0,2,1:T(4,128)S(1)}, f32[3,3,1,33]{3,0,2,1:T(4,128)S(1)}, u32[]{:S(2)}, u32[]{:S(2)}) collective-permute-start(f32[3,3,1,33]{3,0,2,1:T(4,128)S(1)} %get-tuple-element.656), channel_id=1, source_target_pairs={{0,16},{16,32},{32,48},{48,64},{64,80},{80,96},{96,112},{112,128},... | collective-permute-start | bytes 3572 | tf_op jit(solution)/shard_map/ppermute | solution.py:19
  239.5 6.8 %collective-permute-done.19 = f32[3,3,1,33]{3,0,2,1:T(4,128)S(1)} collective-permute-done((f32[3,3,1,33]{3,0,2,1:T(4,128)S(1)}, f32[3,3,1,33]{3,0,2,1:T(4,128)S(1)}, u32[]{:S(2)}, u32[]{:S(2)}) %collective-permute-start.19) | collective-permute-done | bytes 1220 | tf_op jit(solution)/shard_map/ppermute | solution.py:22
  251.1 3.5 collective-permute-done.21
  258.4 3.2 collective-permute-done.23
  263.3 2.6 scatter-add.159
  272.6 2.7 mul.1701
  282.4 4.4 collective-permute-start.24
  288.9 6.8 %collective-permute-done.25 = f32[3,3,1,33]{3,0,2,1:T(4,128)S(1)} collective-permute-done((f32[3,3,1,33]{3,0,2,1:T(4,128)S(1)}, f32[3,3,1,33]{3,0,2,1:T(4,128)S(1)}, u32[]{:S(2)}, u32[]{:S(2)}) %collective-permute-start.25) | collective-permute-done | bytes 1220 | tf_op jit(solution)/shard_map/ppermute | solution.py:22
  295.8 3.5 collective-permute-start.26
  300.7 3.7 collective-permute-done.27
  304.5 3.0 collective-permute-start.28
  308.9 3.2 collective-permute-done.29
  322.1 2.7 mul.1741
  331.9 5.5 %collective-permute-start.30 = (f32[3,3,1,33]{3,0,2,1:T(4,128)S(1)}, f32[3,3,1,33]{3,0,2,1:T(4,128)S(1)}, u32[]{:S(2)}, u32[]{:S(2)}) collective-permute-start(f32[3,3,1,33]{3,0,2,1:T(4,128)S(1)} %get-tuple-element.645), channel_id=1, source_target_pairs={{0,16},{16,32},{32,48},{48,64},{64,80},{80,96},{96,112},{112,128},... | collective-permute-start | bytes 3572 | tf_op jit(solution)/shard_map/ppermute | solution.py:19
  339.5 6.8 %collective-permute-done.31 = f32[3,3,1,33]{3,0,2,1:T(4,128)S(1)} collective-permute-done((f32[3,3,1,33]{3,0,2,1:T(4,128)S(1)}, f32[3,3,1,33]{3,0,2,1:T(4,128)S(1)}, u32[]{:S(2)}, u32[]{:S(2)}) %collective-permute-start.31) | collective-permute-done | bytes 1220 | tf_op jit(solution)/shard_map/ppermute | solution.py:22
  349.2 3.7 collective-permute-done.33
  383.6 5.2 collective-permute-start.36
  390.9 6.8 %collective-permute-done.37 = f32[3,3,1,33]{3,0,2,1:T(4,128)S(1)} collective-permute-done((f32[3,3,1,33]{3,0,2,1:T(4,128)S(1)}, f32[3,3,1,33]{3,0,2,1:T(4,128)S(1)}, u32[]{:S(2)}, u32[]{:S(2)}) %collective-permute-start.37) | collective-permute-done | bytes 1220 | tf_op jit(solution)/shard_map/ppermute | solution.py:22
  400.5 3.7 collective-permute-done.39
  404.3 3.2 collective-permute-start.40
  408.8 3.2 collective-permute-done.41
  412.9 2.3 scatter-add.189
  417.0 2.7 mul.1810
  421.2 2.7 mul.1813
  427.6 2.7 reshape.1884
  432.6 4.8 collective-permute-start.42
  439.4 6.8 %collective-permute-done.43 = f32[3,3,1,33]{3,0,2,1:T(4,128)S(1)} collective-permute-done((f32[3,3,1,33]{3,0,2,1:T(4,128)S(1)}, f32[3,3,1,33]{3,0,2,1:T(4,128)S(1)}, u32[]{:S(2)}, u32[]{:S(2)}) %collective-permute-start.43) | collective-permute-done | bytes 1220 | tf_op jit(solution)/shard_map/ppermute | solution.py:22
  449.6 3.7 collective-permute-done.45
  456.1 3.2 collective-permute-done.47
  462.2 3.3 scatter-add.199
  468.0 2.7 mul.1846
  472.2 2.7 mul.1849
  478.7 2.7 reshape.1886
  483.6 4.8 collective-permute-start.48
  490.5 6.8 %collective-permute-done.49 = f32[3,3,1,33]{3,0,2,1:T(4,128)S(1)} collective-permute-done((f32[3,3,1,33]{3,0,2,1:T(4,128)S(1)}, f32[3,3,1,33]{3,0,2,1:T(4,128)S(1)}, u32[]{:S(2)}, u32[]{:S(2)}) %collective-permute-start.49) | collective-permute-done | bytes 1220 | tf_op jit(solution)/shard_map/ppermute | solution.py:22
  500.4 3.7 collective-permute-done.51
  504.2 2.5 collective-permute-start.52
  508.0 3.2 collective-permute-done.53
  514.1 2.8 scatter-add.209
  528.4 2.8 bitcast_subtract_fusion
  (498 shorter events, 222.6 us)
Async XLA Ops:
  0.6 36.1 %copy-start.16 = (f32[1,1024,256]{2,1,0:T(8,128)S(1)}, f32[1,1024,256]{2,1,0:T(8,128)}, u32[]{:S(2)}) copy-start(f32[1,1024,256]{2,1,0:T(8,128)} %param.89) | copy-start | bytes 3145732
  24.3 34.2 %all-to-all-start = ((f32[16,1,64,256]{3,2,1,0:T(8,128)}), f32[16,1,64,256]{3,2,1,0:T(8,128)S(1)}, u32[]{:S(2)}, u32[]{:S(2)}) async-start(f32[16,1,64,256]{3,2,1,0:T(8,128)} %bitcast_dynamic-update-slice_fusion), calls=%async_computation | async-start | bytes 2097152 | tf_op jit(solution)/shard_map/all_to_all | solution.py:144
  36.7 38.0 %copy-start.44 = (s32[2,3,1,1,1]{1,4,3,2,0:T(1,128)S(1)}, s32[2,3,1,1,1]{1,4,3,2,0:T(1,128)}, u32[]{:S(2)}) copy-start(s32[2,3,1,1,1]{1,4,3,2,0:T(1,128)} %param.90) | copy-start | bytes 76
  58.5 61.5 %copy-start = (f32[16,1,64,256]{3,2,1,0:T(8,128)}, f32[16,1,64,256]{3,2,1,0:T(8,128)S(1)}, u32[]{:S(2)}) copy-start(f32[16,1,64,256]{3,2,1,0:T(8,128)S(1)} %all-to-all-done) | copy-start | bytes 3145732
  58.5 55.3 %all-to-all-start.1 = ((f32[1,1024,256]{2,0,1:T(1,128)}), f32[1,1024,256]{2,0,1:T(1,128)}, u32[]{:S(2)}, u32[]{:S(2)}) async-start(f32[1,1024,256]{2,0,1:T(1,128)} %copy.155), calls=%async_computation.1 | async-start | bytes 2097152 | tf_op jit(solution)/shard_map/all_to_all | solution.py:155
  65.4 10.2 %collective-permute-start = (f32[16,1,256]{2,1,0:T(1,128)S(1)}, f32[16,1,256]{2,1,0:T(1,128)S(1)}, u32[]{:S(2)}, u32[]{:S(2)}) collective-permute-start(f32[16,1,256]{2,1,0:T(1,128)S(1)} %get-tuple-element.579), channel_id=1, source_target_pairs={{0,16},{16,32},{32,48},{48,64},{64,80},{80,96},{96,112},{112,128},... | collective-permute-start | bytes 49160 | tf_op jit(solution)/shard_map/ppermute | solution.py:19
  72.8 14.3 %collective-permute-start.1 = (f32[16,1,256]{2,1,0:T(1,128)S(1)}, f32[16,1,256]{2,1,0:T(1,128)S(1)}, u32[]{:S(2)}, u32[]{:S(2)}) collective-permute-start(f32[16,1,256]{2,1,0:T(1,128)S(1)} %get-tuple-element.580), channel_id=1, source_target_pairs={{16,0},{32,16},{48,32},{64,48},{80,64},{96,80},{112,96},{128,112},... | collective-permute-start | bytes 49160 | tf_op jit(solution)/shard_map/ppermute | solution.py:22
  89.6 17.2 %collective-permute-start.2 = (f32[16,66,1]{1,0,2:T(8,128)S(1)}, f32[16,66,1]{1,0,2:T(8,128)S(1)}, u32[]{:S(2)}, u32[]{:S(2)}) collective-permute-start(f32[16,66,1]{1,0,2:T(8,128)S(1)} %copy.148), channel_id=1, source_target_pairs={{0,4},{4,8},{8,12},{1,5},{5,9},{9,13},{2,6},{6,10},{10,14},{3,7},{... | collective-permute-start | bytes 12680 | tf_op jit(solution)/shard_map/ppermute | solution.py:19
  99.9 7.3 %collective-permute-start.3 = (f32[16,66,1]{1,0,2:T(8,128)S(1)}, f32[16,66,1]{1,0,2:T(8,128)S(1)}, u32[]{:S(2)}, u32[]{:S(2)}) collective-permute-start(f32[16,66,1]{1,0,2:T(8,128)S(1)} %copy.149), channel_id=1, source_target_pairs={{4,0},{8,4},{12,8},{5,1},{9,5},{13,9},{6,2},{10,6},{14,10},{7,3},{... | collective-permute-start | bytes 12680 | tf_op jit(solution)/shard_map/ppermute | solution.py:22
  107.7 8.5 %collective-permute-start.4 = (f32[1,66,258]{2,1,0:T(8,128)S(1)}, f32[1,66,258]{2,1,0:T(8,128)S(1)}, u32[]{:S(2)}, u32[]{:S(2)}) collective-permute-start(f32[1,66,258]{2,1,0:T(8,128)S(1)} %get-tuple-element.566), channel_id=1, source_target_pairs={{1,0},{2,1},{3,2},{5,4},{6,5},{7,6},{9,8},{10,9},{11,10},{13,12},{... | collective-permute-start | bytes 204344 | tf_op jit(solution)/shard_map/ppermute | solution.py:22
  109.0 7.8 %collective-permute-start.5 = (f32[1,66,258]{2,1,0:T(8,128)S(1)}, f32[1,66,258]{2,1,0:T(8,128)}, u32[]{:S(2)}, u32[]{:S(2)}) collective-permute-start(f32[1,66,258]{2,1,0:T(8,128)S(1)} %get-tuple-element.565), channel_id=1, source_target_pairs={{0,1},{1,2},{2,3},{4,5},{5,6},{6,7},{8,9},{9,10},{10,11},{12,13},{... | collective-permute-start | bytes 204344 | tf_op jit(solution)/shard_map/ppermute | solution.py:19
  132.1 30.1 %copy-start.11 = (f32[3,2,64,256]{3,2,1,0:T(8,128)S(1)}, f32[3,2,64,256]{3,2,1,0:T(8,128)}, u32[]{:S(2)}) copy-start(f32[3,2,64,256]{3,2,1,0:T(8,128)} %get-tuple-element.594) | copy-start | bytes 1179652
  132.1 30.1 %copy-start.46 = (f32[3]{0:T(128)S(1)}, f32[3]{0:T(128)}, u32[]{:S(2)}) copy-start(f32[3]{0:T(128)} %get-tuple-element.689) | copy-start | bytes 40
  135.5 5.6 %collective-permute-start.6 = (f32[6,3,1,33]{3,0,2,1:T(8,128)S(1)}, f32[6,3,1,33]{3,0,2,1:T(8,128)S(1)}, u32[]{:S(2)}, u32[]{:S(2)}) collective-permute-start(f32[6,3,1,33]{3,0,2,1:T(8,128)S(1)} %get-tuple-element.597), channel_id=1, source_target_pairs={{0,16},{16,32},{32,48},{48,64},{64,80},{80,96},{96,112},{112,128},... | collective-permute-start | bytes 7136 | tf_op jit(solution)/shard_map/ppermute | solution.py:19
  139.0 8.9 %collective-permute-start.7 = (f32[6,3,1,33]{3,0,2,1:T(8,128)S(1)}, f32[6,3,1,33]{3,0,2,1:T(8,128)S(1)}, u32[]{:S(2)}, u32[]{:S(2)}) collective-permute-start(f32[6,3,1,33]{3,0,2,1:T(8,128)S(1)} %get-tuple-element.598), channel_id=1, source_target_pairs={{16,0},{32,16},{48,32},{64,48},{80,64},{96,80},{112,96},{128,112},... | collective-permute-start | bytes 7136 | tf_op jit(solution)/shard_map/ppermute | solution.py:22
  148.0 10.1 %collective-permute-start.8 = (f32[6,3,11,1]{3,0,2,1:T(8,128)S(1)}, f32[6,3,11,1]{3,0,2,1:T(8,128)S(1)}, u32[]{:S(2)}, u32[]{:S(2)}) collective-permute-start(f32[6,3,11,1]{3,0,2,1:T(8,128)S(1)} %get-tuple-element.629), channel_id=1, source_target_pairs={{0,4},{4,8},{8,12},{1,5},{5,9},{9,13},{2,6},{6,10},{10,14},{3,7},{... | collective-permute-start | bytes 2384 | tf_op jit(solution)/shard_map/ppermute | solution.py:19
  152.4 5.8 %collective-permute-start.9 = (f32[6,3,11,1]{3,0,2,1:T(8,128)S(1)}, f32[6,3,11,1]{3,0,2,1:T(8,128)S(1)}, u32[]{:S(2)}, u32[]{:S(2)}) collective-permute-start(f32[6,3,11,1]{3,0,2,1:T(8,128)S(1)} %get-tuple-element.630), channel_id=1, source_target_pairs={{4,0},{8,4},{12,8},{5,1},{9,5},{13,9},{6,2},{10,6},{14,10},{7,3},{... | collective-permute-start | bytes 2384 | tf_op jit(solution)/shard_map/ppermute | solution.py:22
  153.8 12.8 %collective-permute-start.12 = (f32[16,8,256]{2,1,0:T(8,128)S(1)}, f32[16,8,256]{2,1,0:T(8,128)S(1)}, u32[]{:S(2)}, u32[]{:S(2)}) collective-permute-start(f32[16,8,256]{2,1,0:T(8,128)S(1)} %get-tuple-element.577), channel_id=1, source_target_pairs={{0,16},{16,32},{32,48},{48,64},{64,80},{80,96},{96,112},{112,128},... | collective-permute-start | bytes 393224 | tf_op jit(solution)/shard_map/ppermute | solution.py:19
  155.9 11.7 %collective-permute-start.13 = (f32[16,8,256]{2,1,0:T(8,128)S(1)}, f32[16,8,256]{2,1,0:T(8,128)S(1)}, u32[]{:S(2)}, u32[]{:S(2)}) collective-permute-start(f32[16,8,256]{2,1,0:T(8,128)S(1)} %get-tuple-element.578), channel_id=1, source_target_pairs={{16,0},{32,16},{48,32},{64,48},{80,64},{96,80},{112,96},{128,112},... | collective-permute-start | bytes 393224 | tf_op jit(solution)/shard_map/ppermute | solution.py:22
  158.3 5.6 %collective-permute-start.10 = (f32[6,1,11,35]{3,0,2,1:T(8,128)S(1)}, f32[6,1,11,35]{3,0,2,1:T(8,128)S(1)}, u32[]{:S(2)}, u32[]{:S(2)}) collective-permute-start(f32[6,1,11,35]{3,0,2,1:T(8,128)S(1)} %get-tuple-element.595), channel_id=1, source_target_pairs={{0,1},{1,2},{2,3},{4,5},{5,6},{6,7},{8,9},{9,10},{10,11},{12,13},{... | collective-permute-start | bytes 27728 | tf_op jit(solution)/shard_map/ppermute | solution.py:19
  160.9 5.5 %collective-permute-start.11 = (f32[6,1,11,35]{3,0,2,1:T(8,128)S(1)}, f32[6,1,11,35]{3,0,2,1:T(8,128)S(1)}, u32[]{:S(2)}, u32[]{:S(2)}) collective-permute-start(f32[6,1,11,35]{3,0,2,1:T(8,128)S(1)} %get-tuple-element.596), channel_id=1, source_target_pairs={{1,0},{2,1},{3,2},{5,4},{6,5},{7,6},{9,8},{10,9},{11,10},{13,12},{... | collective-permute-start | bytes 27728 | tf_op jit(solution)/shard_map/ppermute | solution.py:22
  170.3 9.5 %collective-permute-start.14 = (f32[16,80,8]{1,2,0:T(8,128)S(1)}, f32[16,80,8]{1,2,0:T(8,128)S(1)}, u32[]{:S(2)}, u32[]{:S(2)}) collective-permute-start(f32[16,80,8]{1,2,0:T(8,128)S(1)} %copy.156), channel_id=1, source_target_pairs={{0,4},{4,8},{8,12},{1,5},{5,9},{9,13},{2,6},{6,10},{10,14},{3,7},{... | collective-permute-start | bytes 122888 | tf_op jit(solution)/shard_map/ppermute | solution.py:19
  178.5 5.3 %collective-permute-start.15 = (f32[16,80,8]{1,2,0:T(8,128)}, f32[16,80,8]{1,2,0:T(8,128)}, u32[]{:S(2)}, u32[]{:S(2)}) collective-permute-start(f32[16,80,8]{1,2,0:T(8,128)} %copy.157), channel_id=1, source_target_pairs={{4,0},{8,4},{12,8},{5,1},{9,5},{13,9},{6,2},{10,6},{14,10},{7,3},{... | collective-permute-start | bytes 122888 | tf_op jit(solution)/shard_map/ppermute | solution.py:22
  188.2 30.8 %copy-start.13 = (f32[16,8,256]{2,1,0:T(8,128)S(1)}, f32[16,8,256]{2,1,0:T(8,128)}, u32[]{:S(2)}) copy-start(f32[16,8,256]{2,1,0:T(8,128)} %copy-done.12) | copy-start | bytes 393220
  188.2 30.8 %copy-start.15 = (f32[16,8,256]{2,1,0:T(8,128)S(1)}, f32[16,8,256]{2,1,0:T(8,128)}, u32[]{:S(2)}) copy-start(f32[16,8,256]{2,1,0:T(8,128)} %copy-done.14) | copy-start | bytes 393220
  189.6 24.5 %collective-permute-start.16 = (f32[8,80,272]{2,1,0:T(8,128)}, f32[8,80,272]{2,1,0:T(8,128)}, u32[]{:S(2)}, u32[]{:S(2)}) collective-permute-start(f32[8,80,272]{2,1,0:T(8,128)} %get-tuple-element.570), channel_id=1, source_target_pairs={{0,1},{1,2},{2,3},{4,5},{5,6},{6,7},{8,9},{9,10},{10,11},{12,13},{... | collective-permute-start | bytes 2088968 | tf_op jit(solution)/shard_map/ppermute | solution.py:19
  193.2 25.7 %collective-permute-start.17 = (f32[8,80,272]{2,1,0:T(8,128)}, f32[8,80,272]{2,1,0:T(8,128)}, u32[]{:S(2)}, u32[]{:S(2)}) collective-permute-start(f32[8,80,272]{2,1,0:T(8,128)} %get-tuple-element.571), channel_id=1, source_target_pairs={{1,0},{2,1},{3,2},{5,4},{6,5},{7,6},{9,8},{10,9},{11,10},{13,12},{... | collective-permute-start | bytes 2088968 | tf_op jit(solution)/shard_map/ppermute | solution.py:22
  224.5 33.8 %copy-start.30 = (f32[3,9,33]{2,1,0:T(8,128)S(1)}, f32[3,9,33]{2,1,0:T(8,128)}, u32[]{:S(2)}) copy-start(f32[3,9,33]{2,1,0:T(8,128)} %copy.154) | copy-start | bytes 10696
  229.1 10.4 %collective-permute-start.18 = (f32[3,3,1,33]{3,0,2,1:T(4,128)S(1)}, f32[3,3,1,33]{3,0,2,1:T(4,128)S(1)}, u32[]{:S(2)}, u32[]{:S(2)}) collective-permute-start(f32[3,3,1,33]{3,0,2,1:T(4,128)S(1)} %get-tuple-element.656), channel_id=1, source_target_pairs={{0,16},{16,32},{32,48},{48,64},{64,80},{80,96},{96,112},{112,128},... | collective-permute-start | bytes 3572 | tf_op jit(solution)/shard_map/ppermute | solution.py:19
  237.4 8.9 %collective-permute-start.19 = (f32[3,3,1,33]{3,0,2,1:T(4,128)S(1)}, f32[3,3,1,33]{3,0,2,1:T(4,128)S(1)}, u32[]{:S(2)}, u32[]{:S(2)}) collective-permute-start(f32[3,3,1,33]{3,0,2,1:T(4,128)S(1)} %get-tuple-element.657), channel_id=1, source_target_pairs={{16,0},{32,16},{48,32},{64,48},{80,64},{96,80},{112,96},{128,112},... | collective-permute-start | bytes 3572 | tf_op jit(solution)/shard_map/ppermute | solution.py:22
  247.1 4.0 collective-permute-start.20
  248.9 5.7 %collective-permute-start.21 = (f32[3,3,11,1]{3,0,2,1:T(4,128)}, f32[3,3,11,1]{3,0,2,1:T(4,128)S(1)}, u32[]{:S(2)}, u32[]{:S(2)}) collective-permute-start(f32[3,3,11,1]{3,0,2,1:T(4,128)} %get-tuple-element.669), channel_id=1, source_target_pairs={{4,0},{8,4},{12,8},{5,1},{9,5},{13,9},{6,2},{10,6},{14,10},{7,3},{... | collective-permute-start | bytes 1196 | tf_op jit(solution)/shard_map/ppermute | solution.py:22
  254.7 3.6 collective-permute-start.22
  257.0 4.5 collective-permute-start.23
  282.4 6.5 %collective-permute-start.24 = (f32[3,3,1,33]{3,0,2,1:T(4,128)S(1)}, f32[3,3,1,33]{3,0,2,1:T(4,128)S(1)}, u32[]{:S(2)}, u32[]{:S(2)}) collective-permute-start(f32[3,3,1,33]{3,0,2,1:T(4,128)S(1)} %get-tuple-element.649), channel_id=1, source_target_pairs={{0,16},{16,32},{32,48},{48,64},{64,80},{80,96},{96,112},{112,128},... | collective-permute-start | bytes 3572 | tf_op jit(solution)/shard_map/ppermute | solution.py:19
  286.9 8.9 %collective-permute-start.25 = (f32[3,3,1,33]{3,0,2,1:T(4,128)S(1)}, f32[3,3,1,33]{3,0,2,1:T(4,128)S(1)}, u32[]{:S(2)}, u32[]{:S(2)}) collective-permute-start(f32[3,3,1,33]{3,0,2,1:T(4,128)S(1)} %get-tuple-element.650), channel_id=1, source_target_pairs={{16,0},{32,16},{48,32},{64,48},{80,64},{96,80},{112,96},{128,112},... | collective-permute-start | bytes 3572 | tf_op jit(solution)/shard_map/ppermute | solution.py:22
  295.8 4.9 collective-permute-start.26
  299.4 5.0 collective-permute-start.27
  304.5 4.3 collective-permute-start.28
  307.6 4.5 collective-permute-start.29
  331.9 7.5 %collective-permute-start.30 = (f32[3,3,1,33]{3,0,2,1:T(4,128)S(1)}, f32[3,3,1,33]{3,0,2,1:T(4,128)S(1)}, u32[]{:S(2)}, u32[]{:S(2)}) collective-permute-start(f32[3,3,1,33]{3,0,2,1:T(4,128)S(1)} %get-tuple-element.645), channel_id=1, source_target_pairs={{0,16},{16,32},{32,48},{48,64},{64,80},{80,96},{96,112},{112,128},... | collective-permute-start | bytes 3572 | tf_op jit(solution)/shard_map/ppermute | solution.py:19
  337.4 8.9 %collective-permute-start.31 = (f32[3,3,1,33]{3,0,2,1:T(4,128)S(1)}, f32[3,3,1,33]{3,0,2,1:T(4,128)S(1)}, u32[]{:S(2)}, u32[]{:S(2)}) collective-permute-start(f32[3,3,1,33]{3,0,2,1:T(4,128)S(1)} %get-tuple-element.646), channel_id=1, source_target_pairs={{16,0},{32,16},{48,32},{64,48},{80,64},{96,80},{112,96},{128,112},... | collective-permute-start | bytes 3572 | tf_op jit(solution)/shard_map/ppermute | solution.py:22
  346.4 2.8 collective-permute-start.32
  347.9 5.0 collective-permute-start.33
  354.3 6.5 %collective-permute-start.34 = (f32[3,1,11,35]{3,0,2,1:T(4,128)}, f32[3,1,11,35]{3,0,2,1:T(4,128)S(1)}, u32[]{:S(2)}, u32[]{:S(2)}) collective-permute-start(f32[3,1,11,35]{3,0,2,1:T(4,128)} %get-tuple-element.605), channel_id=1, source_target_pairs={{0,1},{1,2},{2,3},{4,5},{5,6},{6,7},{8,9},{9,10},{10,11},{12,13},{... | collective-permute-start | bytes 13868 | tf_op jit(solution)/shard_map/ppermute | solution.py:19
  355.9 4.9 collective-permute-start.35
  383.6 7.2 %collective-permute-start.36 = (f32[3,3,1,33]{3,0,2,1:T(4,128)S(1)}, f32[3,3,1,33]{3,0,2,1:T(4,128)S(1)}, u32[]{:S(2)}, u32[]{:S(2)}) collective-permute-start(f32[3,3,1,33]{3,0,2,1:T(4,128)S(1)} %get-tuple-element.641), channel_id=1, source_target_pairs={{0,16},{16,32},{32,48},{48,64},{64,80},{80,96},{96,112},{112,128},... | collective-permute-start | bytes 3572 | tf_op jit(solution)/shard_map/ppermute | solution.py:19
  388.8 8.9 %collective-permute-start.37 = (f32[3,3,1,33]{3,0,2,1:T(4,128)S(1)}, f32[3,3,1,33]{3,0,2,1:T(4,128)S(1)}, u32[]{:S(2)}, u32[]{:S(2)}) collective-permute-start(f32[3,3,1,33]{3,0,2,1:T(4,128)S(1)} %get-tuple-element.642), channel_id=1, source_target_pairs={{16,0},{32,16},{48,32},{64,48},{80,64},{96,80},{112,96},{128,112},... | collective-permute-start | bytes 3572 | tf_op jit(solution)/shard_map/ppermute | solution.py:22
  397.8 2.7 collective-permute-start.38
  399.2 5.0 collective-permute-start.39
  404.3 4.5 collective-permute-start.40
  407.5 4.5 collective-permute-start.41
  432.6 6.8 %collective-permute-start.42 = (f32[3,3,1,33]{3,0,2,1:T(4,128)S(1)}, f32[3,3,1,33]{3,0,2,1:T(4,128)S(1)}, u32[]{:S(2)}, u32[]{:S(2)}) collective-permute-start(f32[3,3,1,33]{3,0,2,1:T(4,128)S(1)} %get-tuple-element.637), channel_id=1, source_target_pairs={{0,16},{16,32},{32,48},{48,64},{64,80},{80,96},{96,112},{112,128},... | collective-permute-start | bytes 3572 | tf_op jit(solution)/shard_map/ppermute | solution.py:19
  437.4 8.9 %collective-permute-start.43 = (f32[3,3,1,33]{3,0,2,1:T(4,128)S(1)}, f32[3,3,1,33]{3,0,2,1:T(4,128)S(1)}, u32[]{:S(2)}, u32[]{:S(2)}) collective-permute-start(f32[3,3,1,33]{3,0,2,1:T(4,128)S(1)} %get-tuple-element.638), channel_id=1, source_target_pairs={{16,0},{32,16},{48,32},{64,48},{80,64},{96,80},{112,96},{128,112},... | collective-permute-start | bytes 3572 | tf_op jit(solution)/shard_map/ppermute | solution.py:22
  446.3 3.2 collective-permute-start.44
  448.2 5.0 collective-permute-start.45
  453.4 2.7 collective-permute-start.46
  454.8 4.5 collective-permute-start.47
  483.6 6.8 %collective-permute-start.48 = (f32[3,3,1,33]{3,0,2,1:T(4,128)S(1)}, f32[3,3,1,33]{3,0,2,1:T(4,128)S(1)}, u32[]{:S(2)}, u32[]{:S(2)}) collective-permute-start(f32[3,3,1,33]{3,0,2,1:T(4,128)S(1)} %get-tuple-element.633), channel_id=1, source_target_pairs={{0,16},{16,32},{32,48},{48,64},{64,80},{80,96},{96,112},{112,128},... | collective-permute-start | bytes 3572 | tf_op jit(solution)/shard_map/ppermute | solution.py:19
  488.5 8.9 %collective-permute-start.49 = (f32[3,3,1,33]{3,0,2,1:T(4,128)S(1)}, f32[3,3,1,33]{3,0,2,1:T(4,128)S(1)}, u32[]{:S(2)}, u32[]{:S(2)}) collective-permute-start(f32[3,3,1,33]{3,0,2,1:T(4,128)S(1)} %get-tuple-element.634), channel_id=1, source_target_pairs={{16,0},{32,16},{48,32},{64,48},{80,64},{96,80},{112,96},{128,112},... | collective-permute-start | bytes 3572 | tf_op jit(solution)/shard_map/ppermute | solution.py:22
  497.4 3.0 collective-permute-start.50
  499.1 5.0 collective-permute-start.51
  504.2 3.8 collective-permute-start.52
  506.7 4.5 collective-permute-start.53
  (40 other events, 233.1 us)
